TPU v7x, 256 devices: a whole 4x4x8 slice. The times are simulated.
256 devices in a mesh: view: 16 (over z, y_hi), row: 16 (over x, y_lo, core).
Axes of the slice: x: 4, y: 4 (y_hi: 2, y_lo: 2; y = y_hi * 2 + y_lo), z: 8, core: 2. Of those that a mesh axis runs over, the one named last changes fastest.
Arguments:
- latent: bfloat16 [1, 16, 32, 72, 1280], P(None, 'view', 'row'), may hold values from -30 to 30
- gn_gain: float32 [1280], replicated, may hold values from 0.25 to 1.75
- gn_bias: float32 [1280], replicated, may hold values from -3 to 3
- cam_idx: int32 [1, 16], P(None, 'view'), may hold values from 0 to 63
- noise_idx: int32 [1], replicated, may hold values from 0 to 999
- cam_table: bfloat16 [64, 2560], replicated, may hold values from -2 to 2
- noise_table: bfloat16 [1000, 2560], replicated, may hold values from -2 to 2
- conv_w: bfloat16 [3, 3, 1280, 1280], P(None, None, None, 'row'), may hold values from -0.0546875 to 0.0546875
- conv_bias: float32 [1280], replicated, may hold values from -3 to 3
- ln_gain: float32 [1280], replicated, may hold values from 0.25 to 1.75
- attn_in: bfloat16 [3, 1280, 1280], P(None, None, 'view'), may hold values from -0.15625 to 0.15625
- attn_out: bfloat16 [1280, 1280], P('view'), may hold values from -0.15625 to 0.15625
- head_scale: float32 [20], replicated, may hold values from 0.4 to 135
Outputs:
- block_out: bfloat16 [1, 16, 32, 72, 1280], P(None, 'view', 'row')
All inputs are finite; a program needn't handle non-finite values.
Results may differ from a plain program's by a relative error of at most 0.02.
Values may be sent and summed in bfloat16 or wider, within the bound.
No kernel may reach another device: no remote copies, remote signals or barrier semaphores. Data moves between devices by JAX's collectives and lax.ppermute only.
A program may use at most 192 MiB of HBM per device.

v0:
```python
import math
import jax
import jax.numpy as jnp
from jax import lax
from jax.sharding import PartitionSpec as P

GROUPS = 32
epsilon = 1e-05


def attend(query, key_block, value, head_scale):
    view_count = query.shape[0]
    item_count = query.shape[2]
    channels = query.shape[3]
    head_count = head_scale.shape[0]
    head_size = channels // head_count
    query_heads = query.reshape(view_count, item_count, head_count, head_size)
    key_heads = key_block.reshape(view_count, item_count, head_count, head_size)
    value_heads = value.reshape(view_count, item_count, head_count, head_size)
    scores = jnp.einsum(
        "vihd,uihd->ihvu", query_heads, key_heads, preferred_element_type=jnp.float32
    )
    scores = scores * (head_scale / math.sqrt(head_size))[None, :, None, None]
    peak_score = jnp.max(scores, axis=-1, keepdims=True)
    exp_scores = jnp.exp(scores - peak_score)
    soft_weights = (exp_scores / jnp.sum(exp_scores, axis=-1, keepdims=True)).astype(jnp.bfloat16)
    mixed = jnp.einsum(
        "ihvu,uihd->vihd", soft_weights, value_heads, preferred_element_type=jnp.float32
    )
    return mixed.astype(jnp.bfloat16).reshape(view_count, 1, item_count, channels)


def send_back(mixed):
    return lax.all_to_all(mixed, VIEW, split_axis=0, concat_axis=1, tiled=True)


def send_out(pixel_major):
    ys = lax.axis_size("vy")
    zs = lax.axis_size("vz")
    local_views = pixel_major.shape[0]
    parts = pixel_major.reshape((local_views, zs, ys) + pixel_major.shape[2:])
    parts = lax.all_to_all(parts, "vy", split_axis=2, concat_axis=0, tiled=True)
    parts = lax.all_to_all(parts, "vz", split_axis=1, concat_axis=1, tiled=True)
    parts = jnp.swapaxes(parts, 0, 1)
    return parts.reshape((zs * ys * local_views, 1) + pixel_major.shape[2:])


def local(
    latent,
    gn_gain,
    gn_bias,
    cam_idx,
    noise_idx,
    cam_table,
    noise_table,
    conv_w,
    conv_bias,
    ln_gain,
    attn_in,
    attn_out,
    head_scale,
):
    samples, local_views, local_rows, local_cols, channels = latent.shape
    width_out = ln_gain.shape[0]
    out_part = conv_w.shape[-1]
    whole = lax.all_gather(latent, ROW, axis=2, tiled=True)
    whole, attn_in = lax.optimization_barrier((whole, attn_in))
    core = lax.axis_index("core")
    half_in = attn_in.shape[1] // 2
    half_out = attn_out.shape[1] // 2
    in_half = lax.dynamic_slice_in_dim(attn_in, core * half_in, half_in, axis=1)
    in_half = lax.all_gather(in_half, VIEW, axis=0, tiled=False)
    out_half = lax.dynamic_slice_in_dim(attn_out, core * half_out, half_out, axis=1)
    view_devices = lax.axis_size(VIEW)
    out_half = jnp.broadcast_to(out_half[None], (view_devices,) + out_half.shape)
    out_half = lax.all_to_all(out_half, VIEW, split_axis=0, concat_axis=0, tiled=True)
    out_half = out_half.reshape(-1, half_out)
    all_rows = whole.shape[2]
    x_float = whole.astype(jnp.float32)
    grouped = x_float.reshape(
        samples, local_views, all_rows, local_cols, GROUPS, channels // GROUPS
    )
    average = jnp.mean(grouped, axis=(2, 3, 5), keepdims=True)
    centred = grouped - average
    variance = jnp.mean(centred * centred, axis=(2, 3, 5), keepdims=True)
    normed = (centred * lax.rsqrt(variance + epsilon)).reshape(x_float.shape)
    cam_film = jnp.take(cam_table, cam_idx, axis=0).astype(jnp.float32)
    noise_film = jnp.take(noise_table, noise_idx, axis=0).astype(jnp.float32)
    film_rows = cam_film + noise_film[:, None, :]
    film_scale = film_rows[:, :, None, None, :channels]
    film_shift = film_rows[:, :, None, None, channels:]
    hidden = (normed * gn_gain + gn_bias) * (1.0 + film_scale) + film_shift
    activated = jax.nn.silu(hidden).astype(jnp.bfloat16)
    out_half, activated = lax.optimization_barrier((out_half, activated))
    swap = [(0, 1), (1, 0)]
    out_other = lax.ppermute(out_half, "core", swap)
    taps = conv_w.shape[1]
    padded = jnp.pad(activated, ((0, 0), (0, 0), (1, 1), (0, 0), (0, 0)))
    tap_sum = None
    for tap_row in range(conv_w.shape[0]):
        rows_in = padded[:, :, tap_row : tap_row + all_rows].reshape(-1, channels)
        weight_row = jnp.transpose(conv_w[tap_row], (1, 0, 2)).reshape(channels, taps * out_part)
        part = jnp.dot(rows_in, weight_row, preferred_element_type=jnp.float32)
        tap_sum = part if tap_sum is None else tap_sum + part
    tap_sum = tap_sum.reshape(samples, local_views, all_rows, local_cols, taps, out_part)
    wide = jnp.pad(tap_sum, ((0, 0), (0, 0), (0, 0), (1, 1), (0, 0), (0, 0)))
    conv_out = (
        wide[:, :, :, 0:local_cols, 0]
        + wide[:, :, :, 1 : local_cols + 1, 1]
        + wide[:, :, :, 2 : local_cols + 2, 2]
    )
    me = lax.axis_index("chip") * lax.axis_size("core") + core
    conv_part = conv_out.astype(jnp.bfloat16)
    conv_rows = lax.all_to_all(conv_part, ROW, split_axis=2, concat_axis=4, tiled=True)
    out_other, conv_rows = lax.optimization_barrier((out_other, conv_rows))
    resid_out = (latent.astype(jnp.float32) + conv_rows.astype(jnp.float32) + conv_bias).astype(
        jnp.bfloat16
    )
    resid_float = resid_out.astype(jnp.float32)
    middle = jnp.mean(resid_float, axis=-1, keepdims=True)
    spread_y = jnp.mean((resid_float - middle) ** 2, axis=-1, keepdims=True)
    normed_y = ((resid_float - middle) * lax.rsqrt(spread_y + epsilon) * ln_gain).astype(
        jnp.bfloat16
    )
    view_devices = lax.axis_size(VIEW)
    per_device = samples * local_rows * local_cols // view_devices
    pixel_major = jnp.moveaxis(normed_y, 1, 0).reshape(
        local_views, view_devices, per_device, width_out
    )
    views = send_out(pixel_major)
    in_half, views = lax.optimization_barrier((in_half, views))
    in_other = lax.ppermute(in_half, "core", swap)
    flat_block = views.reshape(-1, width_out)
    block_mine = lax.dynamic_slice_in_dim(flat_block, core * half_in, half_in, axis=1)
    block_other = lax.dynamic_slice_in_dim(flat_block, (1 - core) * half_in, half_in, axis=1)
    triple_in = jnp.einsum(
        "pc,jmcd->mpjd", block_mine, in_half, preferred_element_type=jnp.float32
    ) + jnp.einsum("pc,jmcd->mpjd", block_other, in_other, preferred_element_type=jnp.float32)
    triple_in = triple_in.astype(jnp.bfloat16).reshape((3,) + views.shape)
    mixed = send_back(attend(triple_in[0], triple_in[1], triple_in[2], head_scale))
    mixed = jnp.moveaxis(
        mixed.reshape(local_views, samples, local_rows, local_cols, width_out), 0, 1
    )
    flat_mixed = mixed.reshape(-1, width_out)
    cols_mine = jnp.dot(flat_mixed, out_half, preferred_element_type=jnp.float32)
    cols_other = jnp.dot(flat_mixed, out_other, preferred_element_type=jnp.float32)
    projected = jnp.where(
        core == 0,
        jnp.concatenate([cols_mine, cols_other], axis=1),
        jnp.concatenate([cols_other, cols_mine], axis=1),
    )
    return (resid_float + projected.reshape(resid_float.shape)).astype(jnp.bfloat16)


ROW = ("chip", "core")
VIEW = ("vz", "vy")


def solution(mesh):
    cores = 2
    split = jax.sharding.Mesh(
        mesh.devices.reshape(mesh.shape["view"] // 2, 2, mesh.shape["row"] // cores, cores),
        ("vz", "vy", "chip", "core"),
    )
    placed = (
        P(None, VIEW, ROW, None, None),
        P(),
        P(),
        P(None, VIEW),
        P(),
        P(),
        P(),
        P(None, None, None, ROW),
        P(),
        P(),
        P(None, None, VIEW),
        P(VIEW, None),
        P(),
    )
    return jax.shard_map(
        local,
        mesh=split,
        in_specs=placed,
        out_specs=P(None, VIEW, ROW, None, None),
        check_vma=False,
    )
```

profile of v0, /device:TPU:2, one launch (start us, length us, event | category | flops | bytes accessed | tf_op | source)
XLA Modules:
  0.0 250.4 jit_solution(865494250867244917)
XLA Ops:
  6.5 0.7 all-gather.4.cloned.1.call-update
  7.3 0.9 constant_dynamic-slice_fusion.1
  8.2 1.3 broadcast_in_dim.26
  9.5 11.2 %all-to-all-start = ((bf16[16,80,640]{2,1,0:T(8,128)(2,1)}), bf16[16,80,640]{2,1,0:T(8,128)(2,1)}, u32[]{:S(2)}, u32[]{:S(2)}) async-start(bf16[16,80,640]{2,1,0:T(8,128)(2,1)} %broadcast_in_dim.26), calls=%async_computation | async-start | bytes 3276800 | tf_op jit(solution)/shard_map/all_to_all | solution.py:76
  22.1 0.8 fusion.43
  23.0 1.8 fusion.52
  24.8 45.9 %all-gather.4.cloned.1.call-done = bf16[1,1,32,72,1280]{4,3,1,0,2:T(8,128)(2,1)} async-done(((bf16[1,1,2,72,1280]{4,3,1,0,2:T(8,128)(2,1)}), bf16[1,1,32,72,1280]{4,3,1,0,2:T(8,128)(2,1)}) %all-gather.4.cloned.1.call-update) | async-done | bytes 5898256 | tf_op jit(solution)/shard_map/all_gather | solution.py:66
  70.6 3.5 %convert_reduce_fusion = f32[1280]{0:T(1024)S(1)} fusion(bf16[1,1,32,72,1280]{4,3,1,0,2:T(8,128)(2,1)} %all-gather.4.cloned.1.call-done), kind=kLoop, calls=%fused_computation.2 | loop fusion | flops 5896960 | bytes 5903360 | tf_op jit(solution)/shard_map/reduce_sum | solution.py:83
  74.2 0.1 reduce_sum.60
  74.3 0.8 constant_dynamic-slice_fusion
  75.1 0.1 reduce_sum.61
  75.2 0.1 sub.41
  75.3 0.1 sub.42
  75.4 4.3 %fusion.3 = f32[1280]{0:T(1024)S(1)} fusion(bf16[1,1,32,72,1280]{4,3,1,0,2:T(8,128)(2,1)} %all-gather.4.cloned.1.call-done, f32[1280]{0:T(1024)S(1)} %sub.42), kind=kLoop, calls=%fused_computation.5 | loop fusion | flops 11795200 | bytes 5908480 | tf_op jit(solution)/shard_map/reduce_sum | solution.py:85
  79.6 0.1 reduce_sum.63
  79.7 0.1 reduce_sum.64
  79.8 0.1 mul.82
  79.9 0.1 mul.83
  80.0 8.4 %multiply_convert_fusion = bf16[1,1,32,72,1280]{4,3,1,0,2:T(8,128)(2,1)} fusion(bf16[1,1,32,72,1280]{4,3,1,0,2:T(8,128)(2,1)} %all-gather.4.cloned.1.call-done, f32[1280]{0:T(1024)S(1)} %get-tuple-element.44, f32[1280]{0:T(1024)S(1)} %get-tuple-element.43, f32[1280]{0:T(1024)S(1)} %copy-done.6, f32[1280]{0:T(1024)S(1)} %copy-done.7, f32[1280]{0:T(1024)S(1)} %mul.83, ...), kind=kLoop, calls=%fused_computation.10 | loop fusion | flops 35389440 | bytes 11827200 | tf_op jit(solution)/shard_map/convert_element_type | solution.py:93
  88.4 0.2 collective-permute-start
  88.6 5.0 %pad_slice_fusion = (bf16[1,1,32,72,1280]{4,3,1,0,2:T(8,128)(2,1)S(1)}, bf16[1,1,32,72,1280]{4,3,1,0,2:T(8,128)(2,1)S(1)}) fusion(bf16[1,1,32,72,1280]{4,3,1,0,2:T(8,128)(2,1)} %multiply_convert_fusion), kind=kLoop, calls=%fused_computation.11 | loop fusion | bytes 17694720 | tf_op jit(solution)/shard_map/slice | solution.py:101
  93.7 1.7 fusion.59
  95.4 0.9 copy-done.2
  96.4 1.8 convolution_add_fusion.1
  98.2 1.8 convolution_add_fusion
  99.9 5.2 %reshape.304 = f32[1,1,32,72,3,80]{3,2,5,4,1,0:T(8,128)} reshape(f32[2304,240]{0,1:T(8,128)S(1)} %convolution_add_fusion) | data formatting | bytes 4423680 | tf_op jit(solution)/shard_map/reshape | solution.py:105
  105.2 2.9 %fusion.35 = bf16[1,1,32,72,80]{3,2,4,1,0:T(8,128)(2,1)S(1)} fusion(f32[1,1,32,72,3,80]{3,2,5,4,1,0:T(8,128)} %reshape.304), kind=kLoop, calls=%fused_computation.49 | loop fusion | flops 552960 | bytes 5611520 | tf_op jit(solution)/shard_map/convert_element_type | solution.py:113
  108.1 0.7 copy.57
  108.9 14.5 %all_to_all.55 = bf16[1,1,32,72,80]{4,3,1,0,2:T(8,128)(2,1)S(1)} all-to-all(bf16[1,1,32,72,80]{4,3,1,0,2:T(8,128)(2,1)S(1)} %copy.57), channel_id=1, replica_groups=mesh['vz'=8,'vy'=2,'chip'=8,'core'=2] {'chip','core'}, dimensions={2} | all-to-all | bytes 737280 | tf_op jit(solution)/shard_map/all_to_all | solution.py:114
  123.4 0.2 copy.92
  123.5 0.6 all_to_all.43
  124.1 0.2 convert_reduce_fusion.1
  124.4 0.3 fusion.27
  124.7 0.3 fusion.29
  124.9 0.2 reshape_reshape_transpose.3
  125.1 0.2 copy.59
  125.3 16.8 %all_to_all.56 = bf16[1,8,2,9,1280]{4,1,3,0,2:T(8,128)(2,1)S(1)} all-to-all(bf16[1,8,2,9,1280]{4,1,3,0,2:T(8,128)(2,1)S(1)} %copy.59), channel_id=1, replica_groups=mesh['vz'=8,'vy'=2,'chip'=8,'core'=2] {'vy'}, dimensions={2} | all-to-all | bytes 737280 | tf_op jit(solution)/shard_map/all_to_all | solution.py:42
  142.2 0.3 copy.60
  142.5 21.6 %all_to_all.57 = bf16[2,8,1,9,1280]{4,0,3,2,1:T(2,128)(2,1)S(1)} all-to-all(bf16[2,8,1,9,1280]{4,0,3,2,1:T(2,128)(2,1)S(1)} %copy.60), channel_id=1, replica_groups=mesh['vz'=8,'vy'=2,'chip'=8,'core'=2] {'vz'}, dimensions={1} | all-to-all | bytes 737280 | tf_op jit(solution)/shard_map/all_to_all | solution.py:43
  164.1 0.3 copy.61
  164.3 0.1 reshape.305
  164.5 20.6 %all-gather.6.cloned.1.call-done = bf16[48,640,80]{1,2,0:T(8,128)(2,1)} async-done(((bf16[3,640,80]{1,2,0:T(8,128)(2,1)}), bf16[48,640,80]{1,2,0:T(8,128)(2,1)}) %all-gather.6.cloned.1.call-update) | async-done | bytes 4915216 | tf_op jit(solution)/shard_map/all_gather | solution.py:72
  185.1 0.1 copy.62
  185.3 0.2 reshape.306
  185.4 5.1 %fusion.37 = f32[16,3,80,144]{2,3,1,0:T(8,128)S(1)} fusion(bf16[16,3,640,80]{2,3,1,0:T(8,128)(2,1)} %bitcast.96, bf16[144,1280]{1,0:T(8,128)(2,1)S(1)} %reshape.306, s32[]{:T(128)S(6)} %select_n.60), kind=kOutput, calls=%fused_computation.52 | convolution fusion | flops 707788800 | bytes 7311364 | tf_op jit(solution)/shard_map/pc,jmcd->mpjd/dot_general | solution.py:136
  190.5 3.1 %collective-permute-done.1 = bf16[16,3,640,80]{2,3,1,0:T(8,128)(2,1)} collective-permute-done((bf16[16,3,640,80]{2,3,1,0:T(8,128)(2,1)}, bf16[16,3,640,80]{2,3,1,0:T(8,128)(2,1)}, u32[]{:S(2)}, u32[]{:S(2)}) %collective-permute-start.1) | collective-permute-done | bytes 4915232 | tf_op jit(solution)/shard_map/ppermute | solution.py:132
  193.7 5.1 %fusion.13 = bf16[3,144,16,80]{3,1,0,2:T(8,128)(2,1)S(1)} fusion(f32[16,3,80,144]{2,3,1,0:T(8,128)S(1)} %fusion.37, bf16[16,3,640,80]{2,3,1,0:T(8,128)(2,1)} %collective-permute-done.1, bf16[144,1280]{1,0:T(8,128)(2,1)S(1)} %reshape.306, s32[]{:T(128)S(6)} %select_n.66), kind=kOutput, calls=%fused_computation.23 | convolution fusion | flops 708894720 | bytes 9744388 | tf_op jit(solution)/shard_map/pc,jmcd->mpjd/dot_general | solution.py:138
  198.7 0.1 fusion.53
  198.9 0.2 copy.64
  199.0 1.3 reshape_squeeze.10
  200.3 0.2 copy.65
  200.4 2.2 reshape_squeeze.11
  202.6 0.2 copy.63
  202.8 2.2 reshape_squeeze.9
  205.0 3.2 %fusion.54 = (f32[9,20,16]{2,1,0:T(8,128)S(1)}, f32[9,20,16,16]{2,3,1,0:T(8,128)}) fusion(bf16[16,9,20,64]{3,2,1,0:T(8,128)(2,1)} %reshape_squeeze.11, bf16[16,9,20,64]{3,2,1,0:T(8,128)(2,1)S(1)} %reshape_squeeze.10, f32[20]{0:T(128)S(1)} %broadcast_multiply_fusion.1), kind=kOutput, calls=%fused_computation.76 | convolution fusion | flops 6036495 | bytes 933200 | tf_op jit(solution)/shard_map/sub | solution.py:25
  208.1 2.1 fusion.18
  210.2 0.2 copy.75
  210.5 1.5 reshape.372
  211.9 4.6 %all-to-all-start.4 = ((bf16[16,1,9,1280]{3,2,1,0:T(8,128)(2,1)}), bf16[16,1,9,1280]{3,2,1,0:T(8,128)(2,1)S(1)}, u32[]{:S(2)}, u32[]{:S(2)}) async-start(bf16[16,1,9,1280]{3,2,1,0:T(8,128)(2,1)} %reshape.372), calls=%async_computation.4 | async-start | bytes 1310720 | tf_op jit(solution)/shard_map/all_to_all | solution.py:34
  216.5 22.1 %all-to-all-done.4 = bf16[16,1,9,1280]{3,2,1,0:T(8,128)(2,1)S(1)} async-done(((bf16[16,1,9,1280]{3,2,1,0:T(8,128)(2,1)}), bf16[16,1,9,1280]{3,2,1,0:T(8,128)(2,1)S(1)}, u32[]{:S(2)}, u32[]{:S(2)}) %all-to-all-start.4) | async-done | bytes 368672 | tf_op jit(solution)/shard_map/all_to_all | solution.py:34
  238.7 0.2 reshape.308
  238.8 1.9 fusion.19
  240.7 1.9 fusion.22
  242.6 0.9 fusion.30
  (29 shorter events, 0.2 us)
Async XLA Ops:
  6.5 67.7 %copy-start = (bf16[3,1280,80]{1,2,0:T(8,128)(2,1)S(1)}, bf16[3,1280,80]{1,2,0:T(8,128)(2,1)}, u32[]{:S(2)}) copy-start(bf16[3,1280,80]{1,2,0:T(8,128)(2,1)} %param.23) | copy-start | bytes 1843204
  6.5 64.1 %all-gather.4.cloned.1.call-start = ((), (), s32[]{:S(2)}) async-start(), calls=%async_computation.5 | async-start | bytes 6266880 | tf_op jit(solution)/shard_map/all_gather | solution.py:66
  9.5 78.9 %all-to-all-start = ((bf16[16,80,640]{2,1,0:T(8,128)(2,1)}), bf16[16,80,640]{2,1,0:T(8,128)(2,1)}, u32[]{:S(2)}, u32[]{:S(2)}) async-start(bf16[16,80,640]{2,1,0:T(8,128)(2,1)} %broadcast_in_dim.26), calls=%async_computation | async-start | bytes 3276800 | tf_op jit(solution)/shard_map/all_to_all | solution.py:76
  20.7 164.4 %all-gather.6.cloned.1.call-start = ((), (), s32[]{:S(2)}) async-start(), calls=%async_computation.6 | async-start | bytes 5222400 | tf_op jit(solution)/shard_map/all_gather | solution.py:72
  74.2 5.8 %copy-start.6 = (f32[1280]{0:T(1024)S(1)}, f32[1280]{0:T(1024)}, u32[]{:S(2)}) copy-start(f32[1280]{0:T(1024)} %param.15) | copy-start | bytes 15364
  74.2 5.8 %copy-start.7 = (f32[1280]{0:T(1024)S(1)}, f32[1280]{0:T(1024)}, u32[]{:S(2)}) copy-start(f32[1280]{0:T(1024)} %param.14) | copy-start | bytes 15364
  88.4 35.7 %collective-permute-start = (bf16[1280,640]{1,0:T(8,128)(2,1)}, bf16[1280,640]{1,0:T(8,128)(2,1)}, u32[]{:S(2)}, u32[]{:S(2)}) collective-permute-start(bf16[1280,640]{1,0:T(8,128)(2,1)} %bitcast), channel_id=1, source_target_pairs={{0,1},{1,0},{2,3},{3,2},{4,5},{5,4},{6,7},{7,6},{8,9},{9,8},{10,11... | collective-permute-start | bytes 4915208 | tf_op jit(solution)/shard_map/ppermute | solution.py:96
  93.7 2.7 %copy-start.2 = (bf16[1,1,32,72,1280]{4,3,1,0,2:T(8,128)(2,1)S(1)}, bf16[1,1,32,72,1280]{4,3,1,0,2:T(8,128)(2,1)}, u32[]{:S(2)}) copy-start(bf16[1,1,32,72,1280]{4,3,1,0,2:T(8,128)(2,1)} %multiply_convert_fusion) | copy-start | bytes 17694724
  105.2 18.9 %copy-start.3 = (bf16[1,1,2,72,1280]{4,3,2,1,0:T(8,128)(2,1)S(1)}, bf16[1,1,2,72,1280]{4,3,2,1,0:T(8,128)(2,1)}, u32[]{:S(2)}) copy-start(bf16[1,1,2,72,1280]{4,3,2,1,0:T(8,128)(2,1)} %param.13) | copy-start | bytes 1105924
  105.2 18.9 %copy-start.4 = (f32[1280]{0:T(1024)S(1)}, f32[1280]{0:T(1024)}, u32[]{:S(2)}) copy-start(f32[1280]{0:T(1024)} %param.21) | copy-start | bytes 15364
  105.2 19.5 %copy-start.5 = (f32[1280]{0:T(1024)S(1)}, f32[1280]{0:T(1024)}, u32[]{:S(2)}) copy-start(f32[1280]{0:T(1024)} %param.22) | copy-start | bytes 15364
  123.4 61.7 %copy-start.8 = (f32[20]{0:T(128)S(1)}, f32[20]{0:T(128)}, u32[]{:S(2)}) copy-start(f32[20]{0:T(128)} %param.25) | copy-start | bytes 244
  185.1 8.5 %collective-permute-start.1 = (bf16[16,3,640,80]{2,3,1,0:T(8,128)(2,1)}, bf16[16,3,640,80]{2,3,1,0:T(8,128)(2,1)}, u32[]{:S(2)}, u32[]{:S(2)}) collective-permute-start(bf16[16,3,640,80]{2,3,1,0:T(8,128)(2,1)} %bitcast.95), channel_id=1, source_target_pairs={{0,1},{1,0},{2,3},{3,2},{4,5},{5,4},{6,7},{7,6},{8,9},{9,8},{10,11... | collective-permute-start | bytes 14745608 | tf_op jit(solution)/shard_map/ppermute | solution.py:132
  210.2 33.3 %copy-start.1 = (bf16[3,1280,80]{1,2,0:T(8,128)(2,1)S(1)}, bf16[3,1280,80]{1,2,0:T(8,128)(2,1)}, u32[]{:S(2)}) copy-start(bf16[3,1280,80]{1,2,0:T(8,128)(2,1)} %param.23) | copy-start | bytes 1843204
  211.9 26.7 %all-to-all-start.4 = ((bf16[16,1,9,1280]{3,2,1,0:T(8,128)(2,1)}), bf16[16,1,9,1280]{3,2,1,0:T(8,128)(2,1)S(1)}, u32[]{:S(2)}, u32[]{:S(2)}) async-start(bf16[16,1,9,1280]{3,2,1,0:T(8,128)(2,1)} %reshape.372), calls=%async_computation.4 | async-start | bytes 1310720 | tf_op jit(solution)/shard_map/all_to_all | solution.py:34
Sparse Core Ops, SparseCore 0:
  9.2 61.3 all-gather.3
  75.2 109.8 all-gather.5
where the time goes:
time: 251 us; the launch traced here: 250 us
  waiting for transfers between devices  92.5 us (37%)
  blocking collectives  53 us (21%)
  local copies, waits for them, and re-layouts  27.4 us (11%)
  matrix products  24.5 us (10%)
  other arithmetic  21.8 us (9%)
  starting transfers between devices  16.1 us (6%)
  between operations  15.1 us (6%)
    all_gather x1, waiting for transfers between devices, local(): whole = lax.all_gather(latent, ROW, axis=2, tiled=True)  45.9 us
    all_to_all x1, waiting for transfers between devices, send_back(): return lax.all_to_all(mixed, VIEW, split_axis=0, concat_axis=1, tiled=True)  22.1 us
    all_to_all x1, blocking collectives, send_out(): parts = lax.all_to_all(parts, 'vz', split_axis=1, concat_axis=1, tiled=True)  21.6 us
    all_gather x1, waiting for transfers between devices, local(): in_half = lax.all_gather(in_half, VIEW, axis=0, tiled=False)  20.6 us
    all_to_all x1, blocking collectives, send_out(): parts = lax.all_to_all(parts, 'vy', split_axis=2, concat_axis=0, tiled=True)  16.8 us
    all_to_all x1, blocking collectives, local(): lax.all_to_all(conv_part, ROW, split_axis=2, concat_axis=4, tiled=True)  14.5 us
    all_to_all x1, starting transfers between devices, local(): lax.all_to_all(out_half, VIEW, split_axis=0, concat_axis=0, tiled=True)  11.2 us
    convert_element_type x1, other arithmetic, local(): activated = jax.nn.silu(hidden).astype(jnp.bfloat16)  8.36 us
  transfers between devices with their start and end apart: 6, of which 4 were waited for; matrix products, arithmetic and copies ran while one was open for 20% of the time, Pallas kernels for 0%

commit v1 on v0

--- a/solution.py
+++ b/solution.py
@@ -63,7 +63,9 @@
     samples, local_views, local_rows, local_cols, channels = latent.shape
     width_out = ln_gain.shape[0]
     out_part = conv_w.shape[-1]
-    whole = lax.all_gather(latent, ROW, axis=2, tiled=True)
+    whole = jnp.concatenate(
+        lax.all_to_all(jnp.stack([latent] * lax.axis_size(ROW)), ROW, 0, 0), axis=2
+    )
     whole, attn_in = lax.optimization_barrier((whole, attn_in))
     core = lax.axis_index("core")
     half_in = attn_in.shape[1] // 2

time: 251 us -> 321 us (1.28)
  waiting for transfers between devices: 92.5 us -> 127 us
  blocking collectives: 53 us -> 79.7 us
  starting transfers between devices: 16.1 us -> 21.7 us
    all_to_all x0 -> x1, waiting for transfers between devices: none -> 63.2 us  [local(): lax.all_to_all(jnp.stack([latent] * lax.axis_size(ROW)), ROW, 0, 0)]
    all_gather x1 -> x0, waiting for transfers between devices: 45.9 us -> none  [local(): whole = lax.all_gather(latent, ROW, axis=2, tiled=True)]
    all_to_all x1, blocking collectives: 14.5 us -> 42.9 us  [local(): lax.all_to_all(conv_part, ROW, split_axis=2, concat_axis=4, tiled=True)]
    all_to_all x1, waiting for transfers between devices: 0.01 us -> 24.5 us  [local(): lax.all_to_all(out_half, VIEW, split_axis=0, concat_axis=0, tiled=True)]
    all_gather x1, waiting for transfers between devices: 20.6 us -> 13.7 us  [local(): in_half = lax.all_gather(in_half, VIEW, axis=0, tiled=False)]
    all_to_all x0 -> x1, starting transfers between devices: none -> 6.76 us  [local(): lax.all_to_all(jnp.stack([latent] * lax.axis_size(ROW)), ROW, 0, 0)]
    another operation x1 -> x2, local copies, waits for them, and re-layouts: 0.17 us -> 4.17 us  [the longest x1 4 us: local(): jnp.stack([latent] * lax.axis_size(ROW))]
  transfers between devices with their start and end apart: 6 -> 6, of which waited for: 4 -> 5; matrix products, arithmetic and copies ran while one was open for 20% -> 15% of each run, Pallas kernels for 0% -> 0%
where the time goes in v1:
time: 321 us; the launch traced here: 320 us
  waiting for transfers between devices  127 us (40%)
  blocking collectives  79.7 us (25%)
  local copies, waits for them, and re-layouts  30.2 us (9%)
  matrix products  24.5 us (8%)
  other arithmetic  21.8 us (7%)
  starting transfers between devices  21.7 us (7%)
  between operations  15.1 us (5%)
    all_to_all x1, waiting for transfers between devices, local(): lax.all_to_all(jnp.stack([latent] * lax.axis_size(ROW)), ROW, 0, 0)  63.2 us
    all_to_all x1, blocking collectives, local(): lax.all_to_all(conv_part, ROW, split_axis=2, concat_axis=4, tiled=True)  42.9 us
    all_to_all x1, waiting for transfers between devices, local(): lax.all_to_all(out_half, VIEW, split_axis=0, concat_axis=0, tiled=True)  24.5 us
    all_to_all x1, waiting for transfers between devices, send_back(): return lax.all_to_all(mixed, VIEW, split_axis=0, concat_axis=1, tiled=True)  22.1 us
    all_to_all x1, blocking collectives, send_out(): parts = lax.all_to_all(parts, 'vz', split_axis=1, concat_axis=1, tiled=True)  21.3 us
    all_to_all x1, blocking collectives, send_out(): parts = lax.all_to_all(parts, 'vy', split_axis=2, concat_axis=0, tiled=True)  15.5 us
    all_gather x1, waiting for transfers between devices, local(): in_half = lax.all_gather(in_half, VIEW, axis=0, tiled=False)  13.7 us
    all_to_all x1, starting transfers between devices, local(): lax.all_to_all(out_half, VIEW, split_axis=0, concat_axis=0, tiled=True)  10.2 us
  transfers between devices with their start and end apart: 6, of which 5 were waited for; matrix products, arithmetic and copies ran while one was open for 15% of the time, Pallas kernels for 0%

profile of v1, /device:TPU:2, one launch (start us, length us, event | category | flops | bytes accessed | tf_op | source)
XLA Modules:
  0.0 319.7 jit_solution(14160330490361481136)
XLA Ops:
  6.5 4.0 %stack.2 = bf16[16,1,1,2,72,1280]{5,4,3,2,1,0:T(8,128)(2,1)} broadcast(bf16[2,72,1280]{2,1,0:T(8,128)(2,1)} %bitcast.103), dimensions={3,4,5} | broadcast | bytes 6266880 | tf_op jit(solution)/shard_map/stack | solution.py:67
  10.5 6.8 %all-to-all-start.1 = ((bf16[16,1,1,2,72,1280]{5,4,3,2,1,0:T(8,128)(2,1)}), bf16[16,1,1,2,72,1280]{5,4,3,2,1,0:T(8,128)(2,1)}, u32[]{:S(2)}, u32[]{:S(2)}) async-start(bf16[16,1,1,2,72,1280]{5,4,3,2,1,0:T(8,128)(2,1)} %stack.2), calls=%async_computation.1 | async-start | bytes 11796480 | tf_op jit(solution)/shard_map/all_to_all | solution.py:67
  18.6 0.8 fusion.43
  19.5 1.6 fusion.52
  21.1 63.2 %all-to-all-done.1 = bf16[16,1,1,2,72,1280]{5,4,3,2,1,0:T(8,128)(2,1)} async-done(((bf16[16,1,1,2,72,1280]{5,4,3,2,1,0:T(8,128)(2,1)}), bf16[16,1,1,2,72,1280]{5,4,3,2,1,0:T(8,128)(2,1)}, u32[]{:S(2)}, u32[]{:S(2)}) %all-to-all-start.1) | async-done | bytes 5898272 | tf_op jit(solution)/shard_map/all_to_all | solution.py:67
  84.3 1.3 broadcast_in_dim.26
  85.6 10.2 %all-to-all-start = ((bf16[16,80,640]{2,1,0:T(8,128)(2,1)}), bf16[16,80,640]{2,1,0:T(8,128)(2,1)}, u32[]{:S(2)}, u32[]{:S(2)}) async-start(bf16[16,80,640]{2,1,0:T(8,128)(2,1)} %broadcast_in_dim.26), calls=%async_computation | async-start | bytes 3276800 | tf_op jit(solution)/shard_map/all_to_all | solution.py:78
  95.9 3.5 %convert_reduce_fusion = f32[1280]{0:T(1024)S(1)} fusion(bf16[1,1,32,72,1280]{4,3,2,1,0:T(8,128)(2,1)} %bitcast.2), kind=kLoop, calls=%fused_computation.2 | loop fusion | flops 5896960 | bytes 5903360 | tf_op jit(solution)/shard_map/reduce_sum | solution.py:85
  99.4 0.1 reduce_sum.60
  99.5 0.8 constant_dynamic-slice_fusion
  100.3 0.1 reduce_sum.61
  100.4 0.1 sub.41
  100.5 0.1 sub.42
  100.6 4.3 %fusion.3 = f32[1280]{0:T(1024)S(1)} fusion(bf16[1,1,32,72,1280]{4,3,2,1,0:T(8,128)(2,1)} %bitcast.2, f32[1280]{0:T(1024)S(1)} %sub.42), kind=kLoop, calls=%fused_computation.5 | loop fusion | flops 11795200 | bytes 5908480 | tf_op jit(solution)/shard_map/reduce_sum | solution.py:87
  104.8 0.1 reduce_sum.63
  104.9 0.1 reduce_sum.64
  105.0 0.1 mul.82
  105.1 0.1 mul.83
  105.2 8.4 %multiply_convert_fusion = bf16[1,1,32,72,1280]{4,3,2,1,0:T(8,128)(2,1)} fusion(bf16[1,1,32,72,1280]{4,3,2,1,0:T(8,128)(2,1)} %bitcast.2, f32[1280]{0:T(1024)S(1)} %get-tuple-element.44, f32[1280]{0:T(1024)S(1)} %get-tuple-element.43, f32[1280]{0:T(1024)S(1)} %copy-done.7, f32[1280]{0:T(1024)S(1)} %copy-done.8, f32[1280]{0:T(1024)S(1)} %mul.83, f32[1280]{0:T(1024)S(1)} %sub.42), kind=kLoop, calls=%fused_computation.10 | loop fusion | flops 35389440 | bytes 11827200 | tf_op jit(solution)/shard_map/convert_element_type | solution.py:95
  113.6 24.5 %all-to-all-done = bf16[16,80,640]{2,1,0:T(8,128)(2,1)} async-done(((bf16[16,80,640]{2,1,0:T(8,128)(2,1)}), bf16[16,80,640]{2,1,0:T(8,128)(2,1)}, u32[]{:S(2)}, u32[]{:S(2)}) %all-to-all-start) | async-done | bytes 1638432 | tf_op jit(solution)/shard_map/all_to_all | solution.py:78
  138.1 5.0 %pad_slice_fusion = (bf16[1,1,32,72,1280]{4,3,2,1,0:T(8,128)(2,1)S(1)}, bf16[1,1,32,72,1280]{4,3,2,1,0:T(8,128)(2,1)S(1)}) fusion(bf16[1,1,32,72,1280]{4,3,2,1,0:T(8,128)(2,1)} %multiply_convert_fusion), kind=kLoop, calls=%fused_computation.11 | loop fusion | bytes 17694720 | tf_op jit(solution)/shard_map/slice | solution.py:103
  143.1 1.7 fusion.59
  144.9 1.0 copy-done.2
  145.8 1.8 convolution_add_fusion.1
  147.6 1.8 convolution_add_fusion
  149.4 5.2 %reshape.311 = f32[1,1,32,72,3,80]{3,2,5,4,1,0:T(8,128)} reshape(f32[2304,240]{0,1:T(8,128)S(1)} %convolution_add_fusion) | data formatting | bytes 4423680 | tf_op jit(solution)/shard_map/reshape | solution.py:107
  154.7 2.9 fusion.35
  157.6 0.7 copy.69
  158.3 42.9 %all_to_all.60 = bf16[1,1,32,72,80]{4,3,1,0,2:T(8,128)(2,1)S(1)} all-to-all(bf16[1,1,32,72,80]{4,3,1,0,2:T(8,128)(2,1)S(1)} %copy.69), channel_id=1, replica_groups=mesh['vz'=8,'vy'=2,'chip'=8,'core'=2] {'chip','core'}, dimensions={2} | all-to-all | bytes 737280 | tf_op jit(solution)/shard_map/all_to_all | solution.py:116
  201.2 0.2 copy.104
  201.4 0.6 all_to_all.47
  202.0 0.2 convert_reduce_fusion.1
  202.2 0.3 fusion.27
  202.5 0.3 fusion.29
  202.8 0.2 reshape_reshape_transpose.3
  202.9 0.2 copy.71
  203.2 15.5 %all_to_all.61 = bf16[1,8,2,9,1280]{4,1,3,0,2:T(8,128)(2,1)S(1)} all-to-all(bf16[1,8,2,9,1280]{4,1,3,0,2:T(8,128)(2,1)S(1)} %copy.71), channel_id=1, replica_groups=mesh['vz'=8,'vy'=2,'chip'=8,'core'=2] {'vy'}, dimensions={2} | all-to-all | bytes 737280 | tf_op jit(solution)/shard_map/all_to_all | solution.py:42
  218.6 0.3 copy.72
  218.9 21.3 %all_to_all.62 = bf16[2,8,1,9,1280]{4,0,3,2,1:T(2,128)(2,1)S(1)} all-to-all(bf16[2,8,1,9,1280]{4,0,3,2,1:T(2,128)(2,1)S(1)} %copy.72), channel_id=1, replica_groups=mesh['vz'=8,'vy'=2,'chip'=8,'core'=2] {'vz'}, dimensions={1} | all-to-all | bytes 737280 | tf_op jit(solution)/shard_map/all_to_all | solution.py:43
  240.2 0.3 copy.73
  240.5 0.1 reshape.312
  240.6 13.7 %all-gather.3.cloned.1.call-done = bf16[48,640,80]{1,2,0:T(8,128)(2,1)} async-done(((bf16[3,640,80]{1,2,0:T(8,128)(2,1)}), bf16[48,640,80]{1,2,0:T(8,128)(2,1)}) %all-gather.3.cloned.1.call-update) | async-done | bytes 4915216 | tf_op jit(solution)/shard_map/all_gather | solution.py:74
  254.4 0.1 copy.74
  254.5 0.2 reshape.313
  254.7 5.1 %fusion.37 = f32[16,3,80,144]{2,3,1,0:T(8,128)S(1)} fusion(bf16[16,3,640,80]{2,3,1,0:T(8,128)(2,1)} %bitcast.97, bf16[144,1280]{1,0:T(8,128)(2,1)S(1)} %reshape.313, s32[]{:T(128)S(6)} %select_n.60), kind=kOutput, calls=%fused_computation.52 | convolution fusion | flops 707788800 | bytes 7311364 | tf_op jit(solution)/shard_map/pc,jmcd->mpjd/dot_general | solution.py:138
  259.8 3.1 collective-permute-done.1
  262.9 5.1 %fusion.13 = bf16[3,144,16,80]{3,1,0,2:T(8,128)(2,1)S(1)} fusion(f32[16,3,80,144]{2,3,1,0:T(8,128)S(1)} %fusion.37, bf16[16,3,640,80]{2,3,1,0:T(8,128)(2,1)} %collective-permute-done.1, bf16[144,1280]{1,0:T(8,128)(2,1)S(1)} %reshape.313, s32[]{:T(128)S(6)} %select_n.66), kind=kOutput, calls=%fused_computation.23 | convolution fusion | flops 708894720 | bytes 9744388 | tf_op jit(solution)/shard_map/pc,jmcd->mpjd/dot_general | solution.py:140
  268.0 0.1 fusion.53
  268.1 0.2 copy.76
  268.3 1.3 reshape_squeeze.10
  269.6 0.2 copy.77
  269.7 2.2 reshape_squeeze.11
  271.9 0.2 copy.75
  272.1 2.2 reshape_squeeze.9
  274.2 3.2 fusion.54
  277.4 2.1 fusion.18
  279.5 0.2 copy.87
  279.7 1.5 reshape.379
  281.2 4.7 %all-to-all-start.5 = ((bf16[16,1,9,1280]{3,2,1,0:T(8,128)(2,1)}), bf16[16,1,9,1280]{3,2,1,0:T(8,128)(2,1)S(1)}, u32[]{:S(2)}, u32[]{:S(2)}) async-start(bf16[16,1,9,1280]{3,2,1,0:T(8,128)(2,1)} %reshape.379), calls=%async_computation.5 | async-start | bytes 1310720 | tf_op jit(solution)/shard_map/all_to_all | solution.py:34
  285.9 22.1 %all-to-all-done.5 = bf16[16,1,9,1280]{3,2,1,0:T(8,128)(2,1)S(1)} async-done(((bf16[16,1,9,1280]{3,2,1,0:T(8,128)(2,1)}), bf16[16,1,9,1280]{3,2,1,0:T(8,128)(2,1)S(1)}, u32[]{:S(2)}, u32[]{:S(2)}) %all-to-all-start.5) | async-done | bytes 368672 | tf_op jit(solution)/shard_map/all_to_all | solution.py:34
  308.0 0.2 reshape.315
  308.2 1.9 fusion.19
  310.1 1.9 fusion.22
  312.0 0.9 fusion.30
  (31 shorter events, 0.2 us)
Async XLA Ops:
  6.5 93.0 %copy-start = (bf16[3,1280,80]{1,2,0:T(8,128)(2,1)S(1)}, bf16[3,1280,80]{1,2,0:T(8,128)(2,1)}, u32[]{:S(2)}) copy-start(bf16[3,1280,80]{1,2,0:T(8,128)(2,1)} %param.23) | copy-start | bytes 1843204
  10.5 9.0 %copy-start.4 = (bf16[80,1280]{1,0:T(8,128)(2,1)S(1)}, bf16[80,1280]{1,0:T(8,128)(2,1)}, u32[]{:S(2)}) copy-start(bf16[80,1280]{1,0:T(8,128)(2,1)} %param.24) | copy-start | bytes 614404
  10.5 73.8 %all-to-all-start.1 = ((bf16[16,1,1,2,72,1280]{5,4,3,2,1,0:T(8,128)(2,1)}), bf16[16,1,1,2,72,1280]{5,4,3,2,1,0:T(8,128)(2,1)}, u32[]{:S(2)}, u32[]{:S(2)}) async-start(bf16[16,1,1,2,72,1280]{5,4,3,2,1,0:T(8,128)(2,1)} %stack.2), calls=%async_computation.1 | async-start | bytes 11796480 | tf_op jit(solution)/shard_map/all_to_all | solution.py:67
  85.6 52.5 %all-to-all-start = ((bf16[16,80,640]{2,1,0:T(8,128)(2,1)}), bf16[16,80,640]{2,1,0:T(8,128)(2,1)}, u32[]{:S(2)}, u32[]{:S(2)}) async-start(bf16[16,80,640]{2,1,0:T(8,128)(2,1)} %broadcast_in_dim.26), calls=%async_computation | async-start | bytes 3276800 | tf_op jit(solution)/shard_map/all_to_all | solution.py:78
  95.8 158.6 %all-gather.3.cloned.1.call-start = ((), (), s32[]{:S(2)}) async-start(), calls=%async_computation.6 | async-start | bytes 5222400 | tf_op jit(solution)/shard_map/all_gather | solution.py:74
  99.4 5.8 %copy-start.7 = (f32[1280]{0:T(1024)S(1)}, f32[1280]{0:T(1024)}, u32[]{:S(2)}) copy-start(f32[1280]{0:T(1024)} %param.15) | copy-start | bytes 15364
  99.4 5.8 %copy-start.8 = (f32[1280]{0:T(1024)S(1)}, f32[1280]{0:T(1024)}, u32[]{:S(2)}) copy-start(f32[1280]{0:T(1024)} %param.14) | copy-start | bytes 15364
  138.1 63.8 %collective-permute-start = (bf16[1280,640]{1,0:T(8,128)(2,1)}, bf16[1280,640]{1,0:T(8,128)(2,1)}, u32[]{:S(2)}, u32[]{:S(2)}) collective-permute-start(bf16[1280,640]{1,0:T(8,128)(2,1)} %bitcast), channel_id=1, source_target_pairs={{0,1},{1,0},{2,3},{3,2},{4,5},{5,4},{6,7},{7,6},{8,9},{9,8},{10,11... | collective-permute-start | bytes 4915208 | tf_op jit(solution)/shard_map/ppermute | solution.py:98
  143.1 2.7 copy-start.2
  154.7 47.3 %copy-start.3 = (bf16[1,1,2,72,1280]{4,3,2,1,0:T(8,128)(2,1)S(1)}, bf16[1,1,2,72,1280]{4,3,2,1,0:T(8,128)(2,1)}, u32[]{:S(2)}) copy-start(bf16[1,1,2,72,1280]{4,3,2,1,0:T(8,128)(2,1)} %param.13) | copy-start | bytes 1105924
  154.7 47.3 %copy-start.5 = (f32[1280]{0:T(1024)S(1)}, f32[1280]{0:T(1024)}, u32[]{:S(2)}) copy-start(f32[1280]{0:T(1024)} %param.21) | copy-start | bytes 15364
  154.7 47.8 %copy-start.6 = (f32[1280]{0:T(1024)S(1)}, f32[1280]{0:T(1024)}, u32[]{:S(2)}) copy-start(f32[1280]{0:T(1024)} %param.22) | copy-start | bytes 15364
  201.2 53.2 %copy-start.9 = (f32[20]{0:T(128)S(1)}, f32[20]{0:T(128)}, u32[]{:S(2)}) copy-start(f32[20]{0:T(128)} %param.25) | copy-start | bytes 244
  254.4 8.5 %collective-permute-start.1 = (bf16[16,3,640,80]{2,3,1,0:T(8,128)(2,1)}, bf16[16,3,640,80]{2,3,1,0:T(8,128)(2,1)}, u32[]{:S(2)}, u32[]{:S(2)}) collective-permute-start(bf16[16,3,640,80]{2,3,1,0:T(8,128)(2,1)} %bitcast.96), channel_id=1, source_target_pairs={{0,1},{1,0},{2,3},{3,2},{4,5},{5,4},{6,7},{7,6},{8,9},{9,8},{10,11... | collective-permute-start | bytes 14745608 | tf_op jit(solution)/shard_map/ppermute | solution.py:134
  279.5 33.4 %copy-start.1 = (bf16[3,1280,80]{1,2,0:T(8,128)(2,1)S(1)}, bf16[3,1280,80]{1,2,0:T(8,128)(2,1)}, u32[]{:S(2)}) copy-start(bf16[3,1280,80]{1,2,0:T(8,128)(2,1)} %param.23) | copy-start | bytes 1843204
  281.2 26.8 %all-to-all-start.5 = ((bf16[16,1,9,1280]{3,2,1,0:T(8,128)(2,1)}), bf16[16,1,9,1280]{3,2,1,0:T(8,128)(2,1)S(1)}, u32[]{:S(2)}, u32[]{:S(2)}) async-start(bf16[16,1,9,1280]{3,2,1,0:T(8,128)(2,1)} %reshape.379), calls=%async_computation.5 | async-start | bytes 1310720 | tf_op jit(solution)/shard_map/all_to_all | solution.py:34
Sparse Core Ops, SparseCore 0:
  100.4 153.9 all-gather.2
